TPU v7x, 256 devices: a whole 4x4x8 slice. The times are simulated.
256 devices in a mesh: seq: 64 (over x, z, core), ch: 4 (over y).
Axes of the slice: x: 4, y: 4, z: 8, core: 2. Of those that a mesh axis runs over, the one named last changes fastest.
Arguments:
- inputs: bfloat16 [8192, 4096], P('seq'), may hold values from -6 to 6
- norm_gain: float32 [4096], replicated, may hold values from 0.1 to 1.9
- in_weight: bfloat16 [4096, 3, 1024], P('seq', None, 'ch'), may hold values from -0.09375 to 0.09375
- short_filter: float32 [3, 3, 1024], P(None, None, 'ch'), may hold values from -4 to 4
- long_filter: float32 [8192, 1024], P('seq', 'ch'), may hold values from -2.2 to 2.2
- conv_bias: float32 [1024], P('ch'), may hold values from -4 to 4
- out_weight: bfloat16 [1024, 4096], P('ch', 'seq'), may hold values from -0.1875 to 0.1875
- out_grad: bfloat16 [8192, 4096], P('seq'), may hold values from -6 to 6
Outputs:
- block_out: bfloat16 [8192, 4096], P('seq', 'ch')
- in_grad: bfloat16 [8192, 4096], P('seq')
- filter_grad: float32 [8192, 1024], P('seq', 'ch')
All inputs are finite; a program needn't handle non-finite values.
Results may differ from a plain program's by a relative error of at most 0.013.
Values may be sent and summed in bfloat16 or wider, within the bound.
No kernel may reach another device: no remote copies, remote signals or barrier semaphores. Data moves between devices by JAX's collectives and lax.ppermute only.
A program may use at most 64 MiB of HBM per device.

v0:
```python
import math
import jax
import jax.numpy as jnp
from jax import lax
from jax.sharding import PartitionSpec as P

epsilon = 1e-05
highest = lax.Precision.HIGHEST


def passed_along(block, axis, distance):
    devices = range(lax.axis_size(axis))
    route = [(i - distance, i) for i in devices if i - distance in devices]
    return lax.ppermute(block, axis, route)


def doubled_gather(block, axis):
    devices = lax.axis_size(axis)
    place = lax.axis_index(axis)
    bits = devices.bit_length() - 1
    assert 1 << bits == devices
    gathered = block
    for bit in reversed(range(bits)):
        route = [(i, i ^ 1 << bit) for i in range(devices)]
        arrived = lax.ppermute(gathered, axis, route)
        lower = place >> bit & 1 == 0
        gathered = jnp.where(lower, jnp.stack([gathered, arrived]), jnp.stack([arrived, gathered]))
    gathered = gathered.transpose(tuple(reversed(range(bits))) + tuple(range(bits, gathered.ndim)))
    return gathered.reshape((devices * block.shape[0],) + block.shape[1:])


def halved_sum(partial, axis):
    devices = lax.axis_size(axis)
    place = lax.axis_index(axis)
    bits = devices.bit_length() - 1
    assert 1 << bits == devices
    rows, width = partial.shape
    share = width // devices
    held = partial.reshape((rows,) + (2,) * bits + (share,))
    held = held.transpose((0,) + tuple(range(bits, 0, -1)) + (bits + 1,)).astype(jnp.float32)
    for bit in range(bits):
        route = [(i, i ^ 1 << bit) for i in range(devices)]
        mine = place >> bit & 1
        kept = lax.dynamic_index_in_dim(held, mine, 1, keepdims=False)
        given = lax.dynamic_index_in_dim(held, 1 - mine, 1, keepdims=False)
        arrived = lax.ppermute(given.astype(jnp.bfloat16), axis, route)
        held = kept + arrived.astype(jnp.float32)
    return held


def to_columns(signals):
    return lax.all_to_all(signals, "seq", split_axis=1, concat_axis=2, tiled=True)


def to_rows(signals):
    count, chans, seq_total = signals.shape
    devices = lax.axis_size("seq")
    local_rows = seq_total // devices
    pieces = signals.reshape(count, chans, devices, local_rows).transpose(2, 0, 1, 3)
    arrived = lax.all_to_all(pieces, "seq", split_axis=0, concat_axis=0, tiled=True)
    return arrived.transpose(1, 3, 0, 2).reshape(count, local_rows, devices * chans)


def turn_table(rows, cols, period, sign):
    turns = jnp.arange(rows, dtype=jnp.int32)[:, None] * jnp.arange(cols, dtype=jnp.int32)[None, :]
    turns = lax.optimization_barrier(turns)
    phases = sign * 2.0 * math.pi / period * (turns % period).astype(jnp.float32)
    return (jnp.cos(phases), jnp.sin(phases))


def fft_sizes(seq_total):
    total = 2 * seq_total
    inner = 1
    while inner * inner < total:
        inner *= 2
    return (total // inner, inner)


def forward_dft(signals):
    count, chans, seq_total = signals.shape
    outer, inner = fft_sizes(seq_total)
    grid = signals.reshape(count, chans, outer // 2, inner)
    cos_out, sin_out = turn_table(outer, outer // 2, outer, 1.0)
    first = jnp.einsum(
        "kn,ucnm->uckm", jnp.concatenate([cos_out, -sin_out], 0), grid, precision=lax.Precision.HIGH
    )
    first_real, first_imag = (first[:, :, :outer], first[:, :, outer:])
    cos_tw, sin_tw = turn_table(outer, inner, outer * inner, 1.0)
    turned_real = first_real * cos_tw + first_imag * sin_tw
    turned_imag = first_imag * cos_tw - first_real * sin_tw
    cos_in, sin_in = turn_table(inner, inner, inner, 1.0)
    rotation = jnp.concatenate(
        [jnp.concatenate([cos_in, -sin_in], 1), jnp.concatenate([sin_in, cos_in], 1)], 0
    )
    joined = jnp.concatenate([turned_real, turned_imag], -1)
    spec = jnp.einsum("uckm,mj->uckj", joined, rotation, precision=lax.Precision.HIGH)
    return (spec[..., :inner], spec[..., inner:])


def inverse_dft(spec_real, spec_imag):
    count, chans, outer, inner = spec_real.shape
    cos_in, sin_in = turn_table(inner, inner, inner, 1.0)
    rotation = jnp.concatenate(
        [jnp.concatenate([cos_in, sin_in], 1), jnp.concatenate([-sin_in, cos_in], 1)], 0
    )
    joined = jnp.concatenate([spec_real, spec_imag], -1)
    back = jnp.einsum("uckj,jm->uckm", joined, rotation, precision=lax.Precision.HIGH)
    back_real, back_imag = (back[..., :inner], back[..., inner:])
    cos_tw, sin_tw = turn_table(outer, inner, outer * inner, 1.0)
    turned_real = back_real * cos_tw - back_imag * sin_tw
    turned_imag = back_imag * cos_tw + back_real * sin_tw
    cos_out, sin_out = turn_table(outer, outer // 2, outer, 1.0)
    grid = jnp.einsum(
        "kn,uckm->ucnm",
        jnp.concatenate([cos_out, -sin_out], 0),
        jnp.concatenate([turned_real, turned_imag], 2),
        precision=lax.Precision.HIGH,
    )
    return grid.reshape(count, chans, outer * inner // 2) / float(outer * inner)


def per_device(
    inputs, norm_gain, in_weight, short_filter, long_filter, conv_bias, out_weight, out_grad
):
    local_rows = inputs.shape[0]
    model_width = inputs.shape[1]
    slab_width = long_filter.shape[1]
    taps = short_filter.shape[1]
    wide_inputs = inputs.astype(jnp.float32)
    inv_rms = lax.rsqrt(jnp.mean(wide_inputs * wide_inputs, axis=1, keepdims=True) + epsilon)
    normed = (wide_inputs * inv_rms * norm_gain).astype(jnp.bfloat16)
    in_panel, out_panel = (
        lax.all_gather(in_weight.reshape(in_weight.shape[0], -1), "seq", axis=0, tiled=True),
        doubled_gather(out_weight.T, "seq").T,
    )
    in_flat = in_panel.reshape(model_width, 3 * slab_width)
    projected = jnp.dot(normed, in_flat, preferred_element_type=jnp.float32)
    projected = projected.astype(jnp.bfloat16).reshape(local_rows, 3, slab_width)
    upper_rim = passed_along(projected[local_rows - (taps - 1) :], "seq", 1)
    extended = jnp.concatenate([upper_rim, projected], 0).astype(jnp.float32)
    mixed = jnp.zeros((local_rows, 3, slab_width), jnp.float32)
    for offset in range(taps):
        begin = taps - 1 - offset
        mixed = mixed + short_filter[:, offset, :][None] * extended[begin : begin + local_rows]
    query_br = mixed[:, 0]
    key_br = mixed[:, 1]
    value_br = mixed[:, 2]
    product = key_br * value_br
    gate_grad = jnp.dot(out_grad, out_panel.T, preferred_element_type=jnp.float32)
    carried = gate_grad * query_br
    filt_real, filt_imag = forward_dft(to_columns(long_filter.T[None]))
    filt_real, filt_imag = (filt_real[0], filt_imag[0])
    columns = to_columns(jnp.stack([product, carried]).transpose(0, 2, 1))
    all_real, all_imag = forward_dft(columns)
    sig_real, grad_real = (all_real[0], all_real[1])
    sig_imag, grad_imag = (all_imag[0], all_imag[1])
    conv_real = sig_real * filt_real - sig_imag * filt_imag
    conv_imag = sig_real * filt_imag + sig_imag * filt_real
    back_real = grad_real * filt_real + grad_imag * filt_imag
    back_imag = grad_imag * filt_real - grad_real * filt_imag
    pair_real = grad_real * sig_real + grad_imag * sig_imag
    pair_imag = grad_imag * sig_real - grad_real * sig_imag
    outs = inverse_dft(
        jnp.stack([conv_real, back_real, pair_real]), jnp.stack([conv_imag, back_imag, pair_imag])
    )
    returned = to_rows(outs)
    conv_out = returned[0]
    back_conv = returned[1]
    filter_grad = returned[2] * float(local_rows * lax.axis_size("seq")) ** (-0.5)
    biased = conv_out + conv_bias * product
    gated = (query_br * biased).astype(jnp.bfloat16)
    partial_out = jnp.dot(gated, out_panel, preferred_element_type=jnp.float32)
    source_grad = back_conv + conv_bias * carried
    mixed_grad = jnp.stack([gate_grad * biased, source_grad * value_br, source_grad * key_br], 1)
    lower_rim = passed_along(mixed_grad[: taps - 1], "seq", -1)
    extended_back = jnp.concatenate([mixed_grad, lower_rim], 0)
    proj_grad = jnp.zeros((local_rows, 3, slab_width), jnp.float32)
    for offset in range(taps):
        proj_grad = (
            proj_grad
            + short_filter[:, offset, :][None] * extended_back[offset : offset + local_rows]
        )
    proj_grad = proj_grad.astype(jnp.bfloat16).reshape(local_rows, 3 * slab_width)
    partial_grad = jnp.dot(proj_grad, in_flat.T, preferred_element_type=jnp.float32)
    ch_size = lax.axis_size("ch")
    feature_share = model_width // ch_size
    partial_inner = jnp.sum(partial_grad * (norm_gain * wide_inputs), axis=1, keepdims=True)
    inner_high = partial_inner.astype(jnp.bfloat16)
    inner_low = (partial_inner - inner_high.astype(jnp.float32)).astype(jnp.bfloat16)
    extra = jnp.concatenate(
        [inner_high, inner_low, jnp.zeros((local_rows, 126), jnp.bfloat16)], axis=1
    )
    payload = jnp.concatenate(
        [
            partial_out.astype(jnp.bfloat16)
            .reshape(local_rows, ch_size, feature_share)
            .transpose(1, 0, 2),
            partial_grad.astype(jnp.bfloat16)
            .reshape(local_rows, ch_size, feature_share)
            .transpose(1, 0, 2),
            jnp.broadcast_to(extra[None], (ch_size, local_rows, 128)),
        ],
        axis=2,
    )
    reduced = lax.psum_scatter(payload, "ch", scatter_dimension=0).astype(jnp.float32)
    summed = reduced[:, :feature_share]
    norm_grad = reduced[:, feature_share : 2 * feature_share]
    inner_at = 2 * feature_share
    inner_term = (
        reduced[:, inner_at : inner_at + 1] + reduced[:, inner_at + 1 : inner_at + 2]
    ) / model_width
    feature_begin = lax.axis_index("ch") * feature_share
    residual = lax.dynamic_slice_in_dim(wide_inputs, feature_begin, feature_share, 1)
    block_out = (residual + summed).astype(jnp.bfloat16)
    gain_share = lax.dynamic_slice_in_dim(norm_gain, feature_begin, feature_share, 0)
    inputs_share = lax.dynamic_slice_in_dim(wide_inputs, feature_begin, feature_share, 1)
    grad_share = lax.dynamic_slice_in_dim(out_grad, feature_begin, feature_share, 1)
    weighted = norm_grad * gain_share
    in_grad_share = (
        grad_share.astype(jnp.float32) + weighted * inv_rms - inputs_share * inv_rms**3 * inner_term
    ).astype(jnp.bfloat16)
    in_grad = (
        doubled_gather(in_grad_share[None], "ch")
        .transpose(1, 0, 2)
        .reshape(local_rows, model_width)
    )
    return (block_out, in_grad, filter_grad)


def solution(mesh):
    return jax.shard_map(
        per_device,
        mesh=mesh,
        in_specs=(
            P("seq", None),
            P(),
            P("seq", None, "ch"),
            P(None, None, "ch"),
            P("seq", "ch"),
            P("ch"),
            P("ch", "seq"),
            P("seq", None),
        ),
        out_specs=(P("seq", "ch"), P("seq", None), P("seq", "ch")),
        check_vma=False,
    )
```

profile of v0, /device:TPU:2, one launch (start us, length us, event | category | flops | bytes accessed | tf_op | source)
XLA Modules:
  0.0 249.4 jit_solution(18105231908628929155)
XLA Ops:
  7.2 1.5 copy.156
  8.8 2.2 collective-permute-start.1
  11.0 1.7 copy.126
  12.6 11.2 %all-to-all-start.1 = ((f32[1,256,128]{2,0,1:T(1,128)}), f32[1,256,128]{2,0,1:T(1,128)}, u32[]{:S(2)}, u32[]{:S(2)}) async-start(f32[1,256,128]{2,0,1:T(1,128)} %bitcast.1), calls=%async_computation.1 | async-start | bytes 262144 | tf_op jit(solution)/shard_map/all_to_all | solution.py:52
  28.5 2.5 %collective-permute-done.2 = bf16[2,64,256]{2,1,0:T(8,128)(2,1)S(1)} collective-permute-done((bf16[2,64,256]{2,1,0:T(8,128)(2,1)S(1)}, bf16[2,64,256]{2,1,0:T(8,128)(2,1)S(1)}, u32[]{:S(2)}, u32[]{:S(2)}) %collective-permute-start.2) | collective-permute-done | bytes 65568 | tf_op jit(solution)/shard_map/ppermute | solution.py:25
  31.0 5.2 %collective-permute-start.3 = (bf16[2,2,64,256]{3,2,0,1:T(8,128)(2,1)S(1)}, bf16[2,2,64,256]{3,2,0,1:T(8,128)(2,1)S(1)}, u32[]{:S(2)}, u32[]{:S(2)}) collective-permute-start(bf16[2,2,64,256]{3,2,0,1:T(8,128)(2,1)S(1)} %maximum_select_fusion.7), channel_id=1, source_target_pairs={{0,32},{4,36},{8,40},{12,44},{16,48},{20,52},{24,56},{28,60},{32,0... | collective-permute-start | bytes 393224 | tf_op jit(solution)/shard_map/ppermute | solution.py:25
  36.3 6.4 %collective-permute-done.3 = bf16[2,2,64,256]{3,2,0,1:T(8,128)(2,1)S(1)} collective-permute-done((bf16[2,2,64,256]{3,2,0,1:T(8,128)(2,1)S(1)}, bf16[2,2,64,256]{3,2,0,1:T(8,128)(2,1)S(1)}, u32[]{:S(2)}, u32[]{:S(2)}) %collective-permute-start.3) | collective-permute-done | bytes 131104 | tf_op jit(solution)/shard_map/ppermute | solution.py:25
  42.7 3.4 %collective-permute-start.4 = (bf16[2,2,2,64,256]{4,3,0,1,2:T(8,128)(2,1)S(1)}, bf16[2,2,2,64,256]{4,3,0,1,2:T(8,128)(2,1)S(1)}, u32[]{:S(2)}, u32[]{:S(2)}) collective-permute-start(bf16[2,2,2,64,256]{4,3,0,1,2:T(8,128)(2,1)S(1)} %maximum_select_fusion.6), channel_id=1, source_target_pairs={{0,16},{4,20},{8,24},{12,28},{16,0},{20,4},{24,8},{28,12},{32,48},... | collective-permute-start | bytes 786440 | tf_op jit(solution)/shard_map/ppermute | solution.py:25
  46.3 11.2 %collective-permute-done.4 = bf16[2,2,2,64,256]{4,3,0,1,2:T(8,128)(2,1)S(1)} collective-permute-done((bf16[2,2,2,64,256]{4,3,0,1,2:T(8,128)(2,1)S(1)}, bf16[2,2,2,64,256]{4,3,0,1,2:T(8,128)(2,1)S(1)}, u32[]{:S(2)}, u32[]{:S(2)}) %collective-permute-start.4) | collective-permute-done | bytes 262176 | tf_op jit(solution)/shard_map/ppermute | solution.py:25
  60.3 11.2 %collective-permute-done.5 = bf16[2,2,2,2,64,256]{5,4,0,1,2,3:T(8,128)(2,1)S(1)} collective-permute-done((bf16[2,2,2,2,64,256]{5,4,0,1,2,3:T(8,128)(2,1)S(1)}, bf16[2,2,2,2,64,256]{5,4,0,1,2,3:T(8,128)(2,1)S(1)}, u32[]{:S(2)}, u32[]{:S(2)}) %collective-permute-start.5) | collective-permute-done | bytes 524320 | tf_op jit(solution)/shard_map/ppermute | solution.py:25
  74.6 25.0 %all-gather.2.cloned.1.call-done = bf16[4096,768]{1,0:T(8,128)(2,1)} async-done(((bf16[64,768]{1,0:T(8,128)(2,1)}), bf16[4096,768]{1,0:T(8,128)(2,1)}) %all-gather.2.cloned.1.call-update) | async-done | bytes 6291472 | tf_op jit(solution)/shard_map/all_gather | solution.py:133
  99.6 3.9 %convolution_convert_fusion.1 = bf16[128,768]{1,0:T(8,128)(2,1)S(1)} fusion(bf16[4096,768]{1,0:T(8,128)(2,1)} %all-gather.2.cloned.1.call-done, bf16[128,4096]{1,0:T(8,128)(2,1)S(1)} %copy-done, f32[4096]{0:T(1024)S(1)} %copy-done.17, f32[128]{0:T(128)S(1)} %get-tuple-element.53), kind=kOutput, calls=%fused_computation.26 | convolution fusion | flops 807501824 | bytes 7553536 | tf_op jit(solution)/shard_map/dot_general | solution.py:137
  104.1 2.1 collective-permute-start
  107.8 3.6 %collective-permute-done = bf16[2,3,256]{2,0,1:T(2,128)(2,1)S(1)} collective-permute-done((bf16[2,3,256]{2,0,1:T(2,128)(2,1)}, bf16[2,3,256]{2,0,1:T(2,128)(2,1)S(1)}, u32[]{:S(2)}, u32[]{:S(2)}) %collective-permute-start) | collective-permute-done | bytes 3104 | tf_op jit(solution)/shard_map/ppermute | solution.py:14
  112.3 1.8 copy.120
  114.1 6.5 %all-to-all-start = ((f32[2,256,128]{2,0,1:T(2,128)}), f32[2,256,128]{2,0,1:T(2,128)}, u32[]{:S(2)}, u32[]{:S(2)}) async-start(f32[2,256,128]{2,0,1:T(2,128)} %copy.120), calls=%async_computation | async-start | bytes 524288 | tf_op jit(solution)/shard_map/all_to_all | solution.py:52
  124.4 2.3 convolution_bitcast_fusion.1
  126.8 5.3 %all-to-all-done = f32[2,256,128]{2,0,1:T(2,128)} async-done(((f32[2,256,128]{2,0,1:T(2,128)}), f32[2,256,128]{2,0,1:T(2,128)}, u32[]{:S(2)}, u32[]{:S(2)}) %all-to-all-start) | async-done | bytes 262176 | tf_op jit(solution)/shard_map/all_to_all | solution.py:52
  132.1 1.6 convolution_bitcast_fusion
  139.3 6.6 %all-to-all-start.2 = ((f32[64,3,4,128]{3,2,1,0:T(4,128)}), f32[64,3,4,128]{3,2,1,0:T(4,128)}, u32[]{:S(2)}, u32[]{:S(2)}) async-start(f32[64,3,4,128]{3,2,1,0:T(4,128)} %copy.131), calls=%async_computation.2 | async-start | bytes 786432 | tf_op jit(solution)/shard_map/all_to_all | solution.py:60
  146.6 13.4 %all-to-all-done.2 = f32[64,3,4,128]{3,2,1,0:T(4,128)} async-done(((f32[64,3,4,128]{3,2,1,0:T(4,128)}), f32[64,3,4,128]{3,2,1,0:T(4,128)}, u32[]{:S(2)}, u32[]{:S(2)}) %all-to-all-start.2) | async-done | bytes 393248 | tf_op jit(solution)/shard_map/all_to_all | solution.py:60
  160.0 1.8 slice_multiply_fusion.6
  161.7 1.7 copy.132
  163.4 1.7 copy.134
  165.1 1.7 copy.135
  167.9 2.9 %collective-permute-start.7 = (f32[2,3,256]{2,0,1:T(2,128)S(1)}, f32[2,3,256]{2,0,1:T(2,128)S(1)}, u32[]{:S(2)}, u32[]{:S(2)}) collective-permute-start(f32[2,3,256]{2,0,1:T(2,128)S(1)} %slice.165), channel_id=1, source_target_pairs={{4,0},{8,4},{12,8},{16,12},{20,16},{24,20},{28,24},{32,28},{36,32}... | collective-permute-start | bytes 18440 | tf_op jit(solution)/shard_map/ppermute | solution.py:14
  172.5 5.0 %fusion.90 = (bf16[128,4096]{1,0:T(8,128)(2,1)S(1)}, f32[128]{0:T(128)S(1)}) fusion(bf16[128,4096]{1,0:T(8,128)(2,1)S(1)} %copy-done, f32[4096]{0:T(1024)S(1)} %copy-done.18, bf16[128,768]{0,1:T(8,128)(2,1)S(1)} %bitcast.206, bf16[4096,768]{1,0:T(8,128)(2,1)} %all-gather.2.cloned.1.call-done), kind=kOutput, calls=%fused_computation.176 | convolution fusion | flops 807927680 | bytes 8602112 | tf_op jit(solution)/shard_map/dot_general | solution.py:184
  180.7 1.6 pad_maximum_fusion
  182.6 32.0 %reduce-scatter.2.cloned.1.call-done = bf16[1,128,2176]{2,1,0:T(8,128)(2,1)} async-done(((bf16[4,128,2176]{2,1,0:T(8,128)(2,1)}), bf16[1,128,2176]{2,1,0:T(8,128)(2,1)}) %reduce-scatter.2.cloned.1.call-update) | async-done | bytes 557072 | tf_op jit(solution)/shard_map/reduce_scatter | solution.py:205
  216.0 1.9 fusion.29
  219.3 8.0 %collective-permute-done.8 = bf16[1,128,1024]{2,1,0:T(8,128)(2,1)S(1)} collective-permute-done((bf16[1,128,1024]{2,1,0:T(8,128)(2,1)S(1)}, bf16[1,128,1024]{2,1,0:T(8,128)(2,1)S(1)}, u32[]{:S(2)}, u32[]{:S(2)}) %collective-permute-start.8) | collective-permute-done | bytes 262176 | tf_op jit(solution)/shard_map/ppermute | solution.py:25
  228.6 11.7 %collective-permute-done.9 = bf16[2,1,128,1024]{3,2,1,0:T(8,128)(2,1)S(1)} collective-permute-done((bf16[2,1,128,1024]{3,2,1,0:T(8,128)(2,1)S(1)}, bf16[2,1,128,1024]{3,2,1,0:T(8,128)(2,1)S(1)}, u32[]{:S(2)}, u32[]{:S(2)}) %collective-permute-start.9) | collective-permute-done | bytes 524320 | tf_op jit(solution)/shard_map/ppermute | solution.py:25
  (137 shorter events, 36.0 us)
Async XLA Ops:
  7.2 92.5 %all-gather.2.cloned.1.call-start = ((), (), s32[]{:S(2)}) async-start(), calls=%async_computation.4 | async-start | bytes 6389760 | tf_op jit(solution)/shard_map/all_gather | solution.py:133
  8.8 16.6 %collective-permute-start.1 = (bf16[64,256]{1,0:T(8,128)(2,1)}, bf16[64,256]{1,0:T(8,128)(2,1)S(1)}, u32[]{:S(2)}, u32[]{:S(2)}) collective-permute-start(bf16[64,256]{1,0:T(8,128)(2,1)} %bitcast.213), channel_id=1, source_target_pairs={{0,128},{4,132},{8,136},{12,140},{16,144},{20,148},{24,152},{28,15... | collective-permute-start | bytes 98312 | tf_op jit(solution)/shard_map/ppermute | solution.py:25
  12.6 101.5 %all-to-all-start.1 = ((f32[1,256,128]{2,0,1:T(1,128)}), f32[1,256,128]{2,0,1:T(1,128)}, u32[]{:S(2)}, u32[]{:S(2)}) async-start(f32[1,256,128]{2,0,1:T(1,128)} %bitcast.1), calls=%async_computation.1 | async-start | bytes 262144 | tf_op jit(solution)/shard_map/all_to_all | solution.py:52
  26.2 4.8 %collective-permute-start.2 = (bf16[2,64,256]{2,1,0:T(8,128)(2,1)S(1)}, bf16[2,64,256]{2,1,0:T(8,128)(2,1)S(1)}, u32[]{:S(2)}, u32[]{:S(2)}) collective-permute-start(bf16[2,64,256]{2,1,0:T(8,128)(2,1)S(1)} %maximum_select_fusion.8), channel_id=1, source_target_pairs={{0,64},{4,68},{8,72},{12,76},{16,80},{20,84},{24,88},{28,92},{32,9... | collective-permute-start | bytes 196616 | tf_op jit(solution)/shard_map/ppermute | solution.py:25
  31.0 11.7 %collective-permute-start.3 = (bf16[2,2,64,256]{3,2,0,1:T(8,128)(2,1)S(1)}, bf16[2,2,64,256]{3,2,0,1:T(8,128)(2,1)S(1)}, u32[]{:S(2)}, u32[]{:S(2)}) collective-permute-start(bf16[2,2,64,256]{3,2,0,1:T(8,128)(2,1)S(1)} %maximum_select_fusion.7), channel_id=1, source_target_pairs={{0,32},{4,36},{8,40},{12,44},{16,48},{20,52},{24,56},{28,60},{32,0... | collective-permute-start | bytes 393224 | tf_op jit(solution)/shard_map/ppermute | solution.py:25
  42.7 14.7 %collective-permute-start.4 = (bf16[2,2,2,64,256]{4,3,0,1,2:T(8,128)(2,1)S(1)}, bf16[2,2,2,64,256]{4,3,0,1,2:T(8,128)(2,1)S(1)}, u32[]{:S(2)}, u32[]{:S(2)}) collective-permute-start(bf16[2,2,2,64,256]{4,3,0,1,2:T(8,128)(2,1)S(1)} %maximum_select_fusion.6), channel_id=1, source_target_pairs={{0,16},{4,20},{8,24},{12,28},{16,0},{20,4},{24,8},{28,12},{32,48},... | collective-permute-start | bytes 786440 | tf_op jit(solution)/shard_map/ppermute | solution.py:25
  57.5 14.0 %collective-permute-start.5 = (bf16[2,2,2,2,64,256]{5,4,0,1,2,3:T(8,128)(2,1)S(1)}, bf16[2,2,2,2,64,256]{5,4,0,1,2,3:T(8,128)(2,1)S(1)}, u32[]{:S(2)}, u32[]{:S(2)}) collective-permute-start(bf16[2,2,2,2,64,256]{5,4,0,1,2,3:T(8,128)(2,1)S(1)} %maximum_select_fusion.3), channel_id=1, source_target_pairs={{0,8},{4,12},{8,0},{12,4},{16,24},{20,28},{24,16},{28,20},{32,40},... | collective-permute-start | bytes 1572872 | tf_op jit(solution)/shard_map/ppermute | solution.py:25
  58.7 1.4 copy-start.7
  58.7 1.4 copy-start.9
  60.3 11.5 %copy-start = (bf16[128,4096]{1,0:T(8,128)(2,1)S(1)}, bf16[128,4096]{1,0:T(8,128)(2,1)}, u32[]{:S(2)}) copy-start(bf16[128,4096]{1,0:T(8,128)(2,1)} %param.8) | copy-start | bytes 3145732
  71.7 2.8 %collective-permute-start.6 = (bf16[2,2,2,2,2,64,256]{6,5,0,1,2,3,4:T(8,128)(2,1)S(1)}, bf16[2,2,2,2,2,64,256]{6,5,0,1,2,3,4:T(8,128)(2,1)S(1)}, u32[]{:S(2)}, u32[]{:S(2)}) collective-permute-start(bf16[2,2,2,2,2,64,256]{6,5,0,1,2,3,4:T(8,128)(2,1)S(1)} %maximum_select_fusion.1), channel_id=1, source_target_pairs={{0,4},{4,0},{8,12},{12,8},{16,20},{20,16},{24,28},{28,24},{32,36},... | collective-permute-start | bytes 3145736 | tf_op jit(solution)/shard_map/ppermute | solution.py:25
  72.6 27.0 %copy-start.22 = (f32[128]{0:T(128)}, f32[128]{0:T(128)S(1)}, u32[]{:S(2)}) copy-start(f32[128]{0:T(128)S(1)} %get-tuple-element.53) | copy-start | bytes 1540
  74.4 25.2 %copy-start.17 = (f32[4096]{0:T(1024)S(1)}, f32[4096]{0:T(1024)}, u32[]{:S(2)}) copy-start(f32[4096]{0:T(1024)} %param.9) | copy-start | bytes 49156
  99.6 6.6 %copy-start.2 = (bf16[128,4096]{1,0:T(8,128)(2,1)S(1)}, bf16[128,4096]{1,0:T(8,128)(2,1)}, u32[]{:S(2)}) copy-start(bf16[128,4096]{1,0:T(8,128)(2,1)} %param.15) | copy-start | bytes 3145732
  104.1 7.2 %collective-permute-start = (bf16[2,3,256]{2,0,1:T(2,128)(2,1)}, bf16[2,3,256]{2,0,1:T(2,128)(2,1)S(1)}, u32[]{:S(2)}, u32[]{:S(2)}) collective-permute-start(bf16[2,3,256]{2,0,1:T(2,128)(2,1)} %bitcast.6), channel_id=1, source_target_pairs={{0,4},{4,8},{8,12},{12,16},{16,20},{20,24},{24,28},{28,32},{32,36}... | collective-permute-start | bytes 9224 | tf_op jit(solution)/shard_map/ppermute | solution.py:14
  107.7 3.8 %copy-start.3 = (f32[128,256]{1,0:T(8,128)S(1)}, f32[128,256]{1,0:T(8,128)}, u32[]{:S(2)}) copy-start(f32[128,256]{1,0:T(8,128)} %convolution_bitcast_fusion.3) | copy-start | bytes 393220
  114.1 17.9 %all-to-all-start = ((f32[2,256,128]{2,0,1:T(2,128)}), f32[2,256,128]{2,0,1:T(2,128)}, u32[]{:S(2)}, u32[]{:S(2)}) async-start(f32[2,256,128]{2,0,1:T(2,128)} %copy.120), calls=%async_computation | async-start | bytes 524288 | tf_op jit(solution)/shard_map/all_to_all | solution.py:52
  132.1 2.7 %copy-start.4 = (f32[128,128]{1,0:T(8,128)S(1)}, f32[128,128]{1,0:T(8,128)}, u32[]{:S(2)}) copy-start(f32[128,128]{1,0:T(8,128)} %get-tuple-element.42) | copy-start | bytes 196612
  132.1 2.7 %copy-start.5 = (f32[128,128]{1,0:T(8,128)S(1)}, f32[128,128]{1,0:T(8,128)}, u32[]{:S(2)}) copy-start(f32[128,128]{1,0:T(8,128)} %get-tuple-element.44) | copy-start | bytes 196612
  132.1 2.7 %copy-start.6 = (f32[128,128]{1,0:T(8,128)S(1)}, f32[128,128]{1,0:T(8,128)}, u32[]{:S(2)}) copy-start(f32[128,128]{1,0:T(8,128)} %get-tuple-element.46) | copy-start | bytes 196612
  134.7 1.1 copy-start.1
  137.6 29.1 %copy-start.19 = (f32[256]{0:T(256)S(1)}, f32[256]{0:T(256)}, u32[]{:S(2)}) copy-start(f32[256]{0:T(256)} %param.13) | copy-start | bytes 3076
  139.3 20.7 %all-to-all-start.2 = ((f32[64,3,4,128]{3,2,1,0:T(4,128)}), f32[64,3,4,128]{3,2,1,0:T(4,128)}, u32[]{:S(2)}, u32[]{:S(2)}) async-start(f32[64,3,4,128]{3,2,1,0:T(4,128)} %copy.131), calls=%async_computation.2 | async-start | bytes 786432 | tf_op jit(solution)/shard_map/all_to_all | solution.py:60
  145.9 68.7 %reduce-scatter.2.cloned.1.call-start = ((), (), s32[]{:S(2)}) async-start(), calls=%async_computation.5 | async-start | bytes 2785280 | tf_op jit(solution)/shard_map/reduce_scatter | solution.py:205
  166.7 4.1 %copy-start.15 = (f32[128,1,256]{2,0,1:T(8,128)S(1)}, f32[128,1,256]{2,0,1:T(8,128)}, u32[]{:S(2)}) copy-start(f32[128,1,256]{2,0,1:T(8,128)} %copy.132) | copy-start | bytes 393220
  167.9 4.2 %collective-permute-start.7 = (f32[2,3,256]{2,0,1:T(2,128)S(1)}, f32[2,3,256]{2,0,1:T(2,128)S(1)}, u32[]{:S(2)}, u32[]{:S(2)}) collective-permute-start(f32[2,3,256]{2,0,1:T(2,128)S(1)} %slice.165), channel_id=1, source_target_pairs={{4,0},{8,4},{12,8},{16,12},{20,16},{24,20},{28,24},{32,28},{36,32}... | collective-permute-start | bytes 18440 | tf_op jit(solution)/shard_map/ppermute | solution.py:14
  177.5 3.1 %copy-start.20 = (bf16[128]{0:T(256)(128)(2,1)S(1)}, bf16[128]{0:T(256)(128)(2,1)}, u32[]{:S(2)}) copy-start(bf16[128]{0:T(256)(128)(2,1)} %pad.17.clone) | copy-start | bytes 772
  182.3 33.6 %copy-start.21 = (f32[128]{0:T(128)S(1)}, f32[128]{0:T(128)}, u32[]{:S(2)}) copy-start(f32[128]{0:T(128)} %get-tuple-element.52) | copy-start | bytes 1540
  182.4 33.6 %copy-start.23 = (f32[128]{0:T(128)S(1)}, f32[128]{0:T(128)}, u32[]{:S(2)}) copy-start(f32[128]{0:T(128)} %copy-done.22) | copy-start | bytes 1540
  215.8 12.0 %copy-start.16 = (f32[1,128,64,4]{1,3,0,2:T(4,128)S(1)}, f32[1,128,64,4]{1,3,0,2:T(4,128)}, u32[]{:S(2)}) copy-start(f32[1,128,64,4]{1,3,0,2:T(4,128)} %get-tuple-element.35) | copy-start | bytes 393220
  217.9 9.5 %collective-permute-start.8 = (bf16[1,128,1024]{2,1,0:T(8,128)(2,1)S(1)}, bf16[1,128,1024]{2,1,0:T(8,128)(2,1)S(1)}, u32[]{:S(2)}, u32[]{:S(2)}) collective-permute-start(bf16[1,128,1024]{2,1,0:T(8,128)(2,1)S(1)} %bitcast.192), channel_id=1, source_target_pairs={{0,2},{1,3},{2,0},{3,1},{4,6},{5,7},{6,4},{7,5},{8,10},{9,11},{10,... | collective-permute-start | bytes 786440 | tf_op jit(solution)/shard_map/ppermute | solution.py:25
  227.5 12.8 %collective-permute-start.9 = (bf16[2,1,128,1024]{3,2,1,0:T(8,128)(2,1)S(1)}, bf16[2,1,128,1024]{3,2,1,0:T(8,128)(2,1)S(1)}, u32[]{:S(2)}, u32[]{:S(2)}) collective-permute-start(bf16[2,1,128,1024]{3,2,1,0:T(8,128)(2,1)S(1)} %maximum_select_fusion.5), channel_id=1, source_target_pairs={{0,1},{1,0},{2,3},{3,2},{4,5},{5,4},{6,7},{7,6},{8,9},{9,8},{10,11... | collective-permute-start | bytes 1572872 | tf_op jit(solution)/shard_map/ppermute | solution.py:25
  (7 other events, 5.3 us)
Sparse Core Ops, SparseCore 0:
  11.3 88.2 all-gather.1
  182.5 32.1 reduce-scatter.1
where the time goes:
time: 251 us; the launch traced here: 249 us
  waiting for transfers between devices  132 us (53%)
  starting transfers between devices  42.9 us (17%)
  local copies, waits for them, and re-layouts  22.1 us (9%)
  other arithmetic  18.8 us (7%)
  matrix products  18.6 us (7%)
  between operations  14.7 us (6%)
    ppermute x8, waiting for transfers between devices, doubled_gather(): arrived = lax.ppermute(gathered, axis, route)  52.5 us
    reduce_scatter x1, waiting for transfers between devices, per_device(): lax.psum_scatter(payload, 'ch', scatter_dimension=0).astype(jnp.float32)  32 us
    all_gather x1, waiting for transfers between devices, per_device(): lax.all_gather(in_weight.reshape(in_weight.shape[0], -1), 'seq', axis=0,...  25 us
    all_to_all x2, starting transfers between devices, to_columns(): lax.all_to_all(signals, 'seq', split_axis=1, concat_axis=2, tiled=True)  17.7 us
    ppermute x8, starting transfers between devices, doubled_gather(): arrived = lax.ppermute(gathered, axis, route)  13.5 us
    all_to_all x1, waiting for transfers between devices, to_rows(): lax.all_to_all(pieces, 'seq', split_axis=0, concat_axis=0, tiled=True)  13.4 us
    all_to_all x1, starting transfers between devices, to_rows(): lax.all_to_all(pieces, 'seq', split_axis=0, concat_axis=0, tiled=True)  6.64 us
    all_to_all x2, waiting for transfers between devices, to_columns(): lax.all_to_all(signals, 'seq', split_axis=1, concat_axis=2, tiled=True)  5.28 us
  transfers between devices with their start and end apart: 15, of which 13 were waited for; matrix products, arithmetic and copies ran while one was open for 11% of the time, Pallas kernels for 0%

commit v1 on v0

--- a/solution.py
+++ b/solution.py
@@ -6,6 +6,15 @@
 
 epsilon = 1e-05
 highest = lax.Precision.HIGHEST
+
+
+def carry_wires_for(base_x):
+    a_name = "seq"
+    n_all = lax.axis_size(a_name)
+    all_blocks = tuple((n_all if ix == 0 else 1 for ix in range(base_x.ndim)))
+    return lax.all_to_all(
+        jnp.tile(base_x, all_blocks), a_name, split_axis=0, concat_axis=0, tiled=True
+    )
 
 
 def passed_along(block, axis, distance):
@@ -130,7 +139,7 @@
     inv_rms = lax.rsqrt(jnp.mean(wide_inputs * wide_inputs, axis=1, keepdims=True) + epsilon)
     normed = (wide_inputs * inv_rms * norm_gain).astype(jnp.bfloat16)
     in_panel, out_panel = (
-        lax.all_gather(in_weight.reshape(in_weight.shape[0], -1), "seq", axis=0, tiled=True),
+        carry_wires_for(in_weight.reshape(in_weight.shape[0], -1)),
         doubled_gather(out_weight.T, "seq").T,
     )
     in_flat = in_panel.reshape(model_width, 3 * slab_width)

time: 251 us -> 364 us (1.45)
  waiting for transfers between devices: 132 us -> 235 us
  starting transfers between devices: 42.9 us -> 51.6 us
    ppermute x8, waiting for transfers between devices: 52.5 us -> 181 us  [doubled_gather(): arrived = lax.ppermute(gathered, axis, route)]
    all_gather x1 -> x0, waiting for transfers between devices: 25 us -> none  [per_device(): lax.all_gather(in_weight.reshape(in_weight.shape[0], -1), 'seq', axis=0,...]
    all_to_all x0 -> x1, starting transfers between devices: none -> 12.3 us  [carry_wires_for(): lax.all_to_all(jnp.tile(base_x, all_blocks), a_name, split_axis=0, concat...]
    ppermute x8, starting transfers between devices: 13.5 us -> 8.18 us  [doubled_gather(): arrived = lax.ppermute(gathered, axis, route)]
    another operation x0 -> x2, local copies, waits for them, and re-layouts: none -> 4.34 us  [carry_wires_for(): jnp.tile(base_x, all_blocks)]
  transfers between devices with their start and end apart: 15 -> 15, of which waited for: 13 -> 12; matrix products, arithmetic and copies ran while one was open for 11% -> 7% of each run, Pallas kernels for 0% -> 0%
where the time goes in v1:
time: 364 us; the launch traced here: 363 us
  waiting for transfers between devices  235 us (65%)
  starting transfers between devices  51.6 us (14%)
  local copies, waits for them, and re-layouts  24.5 us (7%)
  matrix products  19.6 us (5%)
  other arithmetic  16.9 us (5%)
  between operations  14.8 us (4%)
    ppermute x8, waiting for transfers between devices, doubled_gather(): arrived = lax.ppermute(gathered, axis, route)  181 us
    reduce_scatter x1, waiting for transfers between devices, per_device(): lax.psum_scatter(payload, 'ch', scatter_dimension=0).astype(jnp.float32)  31.8 us
    all_to_all x2, starting transfers between devices, to_columns(): lax.all_to_all(signals, 'seq', split_axis=1, concat_axis=2, tiled=True)  19.6 us
    all_to_all x1, waiting for transfers between devices, to_rows(): lax.all_to_all(pieces, 'seq', split_axis=0, concat_axis=0, tiled=True)  13.3 us
    all_to_all x1, starting transfers between devices, carry_wires_for(): lax.all_to_all(jnp.tile(base_x, all_blocks), a_name, split_axis=0, concat...  12.3 us
    ppermute x8, starting transfers between devices, doubled_gather(): arrived = lax.ppermute(gathered, axis, route)  8.18 us
  transfers between devices with their start and end apart: 15, of which 12 were waited for; matrix products, arithmetic and copies ran while one was open for 7% of the time, Pallas kernels for 0%

profile of v1, /device:TPU:2, one launch (start us, length us, event | category | flops | bytes accessed | tf_op | source)
XLA Modules:
  0.0 362.6 jit_solution(17371574400792910458)
XLA Ops:
  8.1 3.4 tile.9
  11.5 12.3 %all-to-all-start = ((bf16[64,64,768]{2,1,0:T(8,128)(2,1)}), bf16[64,64,768]{2,1,0:T(8,128)(2,1)}, u32[]{:S(2)}, u32[]{:S(2)}) async-start(bf16[64,64,768]{2,1,0:T(8,128)(2,1)} %tile.9), calls=%async_computation | async-start | bytes 12582912 | tf_op jit(solution)/shard_map/all_to_all | solution.py:15
  23.9 2.4 collective-permute-start.1
  26.9 14.4 %collective-permute-done.1 = bf16[64,256]{1,0:T(8,128)(2,1)S(1)} collective-permute-done((bf16[64,256]{1,0:T(8,128)(2,1)S(1)}, bf16[64,256]{1,0:T(8,128)(2,1)S(1)}, u32[]{:S(2)}, u32[]{:S(2)}) %collective-permute-start.1) | collective-permute-done | bytes 32800 | tf_op jit(solution)/shard_map/ppermute | solution.py:34
  41.9 4.3 %collective-permute-done.2 = bf16[2,64,256]{2,1,0:T(8,128)(2,1)S(1)} collective-permute-done((bf16[2,64,256]{2,1,0:T(8,128)(2,1)S(1)}, bf16[2,64,256]{2,1,0:T(8,128)(2,1)S(1)}, u32[]{:S(2)}, u32[]{:S(2)}) %collective-permute-start.2) | collective-permute-done | bytes 65568 | tf_op jit(solution)/shard_map/ppermute | solution.py:34
  46.2 2.6 collective-permute-start.3
  48.8 121.6 %collective-permute-done.3 = bf16[2,2,64,256]{3,2,0,1:T(8,128)(2,1)S(1)} collective-permute-done((bf16[2,2,64,256]{3,2,0,1:T(8,128)(2,1)S(1)}, bf16[2,2,64,256]{3,2,0,1:T(8,128)(2,1)S(1)}, u32[]{:S(2)}, u32[]{:S(2)}) %collective-permute-start.3) | collective-permute-done | bytes 131104 | tf_op jit(solution)/shard_map/ppermute | solution.py:34
  171.3 11.5 %collective-permute-done.4 = bf16[2,2,2,64,256]{4,3,0,1,2:T(8,128)(2,1)S(1)} collective-permute-done((bf16[2,2,2,64,256]{4,3,0,1,2:T(8,128)(2,1)S(1)}, bf16[2,2,2,64,256]{4,3,0,1,2:T(8,128)(2,1)S(1)}, u32[]{:S(2)}, u32[]{:S(2)}) %collective-permute-start.4) | collective-permute-done | bytes 262176 | tf_op jit(solution)/shard_map/ppermute | solution.py:34
  186.4 8.1 %collective-permute-done.5 = bf16[2,2,2,2,64,256]{5,4,0,1,2,3:T(8,128)(2,1)S(1)} collective-permute-done((bf16[2,2,2,2,64,256]{5,4,0,1,2,3:T(8,128)(2,1)S(1)}, bf16[2,2,2,2,64,256]{5,4,0,1,2,3:T(8,128)(2,1)S(1)}, u32[]{:S(2)}, u32[]{:S(2)}) %collective-permute-start.5) | collective-permute-done | bytes 524320 | tf_op jit(solution)/shard_map/ppermute | solution.py:34
  197.5 9.9 %all-to-all-start.2 = ((f32[1,256,128]{2,0,1:T(1,128)}), f32[1,256,128]{2,0,1:T(1,128)}, u32[]{:S(2)}, u32[]{:S(2)}) async-start(f32[1,256,128]{2,0,1:T(1,128)} %bitcast.1), calls=%async_computation.2 | async-start | bytes 262144 | tf_op jit(solution)/shard_map/all_to_all | solution.py:61
  207.5 3.9 %convolution_convert_fusion.1 = bf16[128,768]{1,0:T(8,128)(2,1)S(1)} fusion(bf16[4096,768]{1,0:T(8,128)(2,1)} %bitcast.6, bf16[128,4096]{1,0:T(8,128)(2,1)S(1)} %copy-done, f32[4096]{0:T(1024)S(1)} %copy-done.24, f32[128]{0:T(128)S(1)} %get-tuple-element.53), kind=kOutput, calls=%fused_computation.26 | convolution fusion | flops 807501824 | bytes 7553536 | tf_op jit(solution)/shard_map/dot_general | solution.py:146
  212.0 2.0 collective-permute-start
  215.5 3.7 %collective-permute-done = bf16[2,3,256]{2,0,1:T(2,128)(2,1)S(1)} collective-permute-done((bf16[2,3,256]{2,0,1:T(2,128)(2,1)}, bf16[2,3,256]{2,0,1:T(2,128)(2,1)S(1)}, u32[]{:S(2)}, u32[]{:S(2)}) %collective-permute-start) | collective-permute-done | bytes 3104 | tf_op jit(solution)/shard_map/ppermute | solution.py:23
  220.2 1.8 copy.120
  221.9 9.6 %all-to-all-start.1 = ((f32[2,256,128]{2,0,1:T(2,128)}), f32[2,256,128]{2,0,1:T(2,128)}, u32[]{:S(2)}, u32[]{:S(2)}) async-start(f32[2,256,128]{2,0,1:T(2,128)} %copy.120), calls=%async_computation.1 | async-start | bytes 524288 | tf_op jit(solution)/shard_map/all_to_all | solution.py:61
  235.4 2.3 convolution_bitcast_fusion.1
  237.7 5.3 %all-to-all-done.1 = f32[2,256,128]{2,0,1:T(2,128)} async-done(((f32[2,256,128]{2,0,1:T(2,128)}), f32[2,256,128]{2,0,1:T(2,128)}, u32[]{:S(2)}, u32[]{:S(2)}) %all-to-all-start.1) | async-done | bytes 262176 | tf_op jit(solution)/shard_map/all_to_all | solution.py:61
  243.0 1.6 convolution_bitcast_fusion
  250.2 6.6 %all-to-all-start.3 = ((f32[64,3,4,128]{3,2,1,0:T(4,128)}), f32[64,3,4,128]{3,2,1,0:T(4,128)}, u32[]{:S(2)}, u32[]{:S(2)}) async-start(f32[64,3,4,128]{3,2,1,0:T(4,128)} %copy.131), calls=%async_computation.3 | async-start | bytes 786432 | tf_op jit(solution)/shard_map/all_to_all | solution.py:69
  257.6 13.3 %all-to-all-done.3 = f32[64,3,4,128]{3,2,1,0:T(4,128)} async-done(((f32[64,3,4,128]{3,2,1,0:T(4,128)}), f32[64,3,4,128]{3,2,1,0:T(4,128)}, u32[]{:S(2)}, u32[]{:S(2)}) %all-to-all-start.3) | async-done | bytes 393248 | tf_op jit(solution)/shard_map/all_to_all | solution.py:69
  270.9 1.8 slice_multiply_fusion.6
  272.7 1.7 copy.135
  274.4 1.7 copy.134
  278.5 2.8 collective-permute-start.7
  281.3 1.7 copy.132
  283.0 1.8 convolution_convert_fusion
  286.0 5.0 %fusion.90 = (bf16[128,4096]{1,0:T(8,128)(2,1)S(1)}, f32[128]{0:T(128)S(1)}) fusion(bf16[128,4096]{1,0:T(8,128)(2,1)S(1)} %copy-done, f32[4096]{0:T(1024)S(1)} %copy-done.25, bf16[128,768]{0,1:T(8,128)(2,1)S(1)} %bitcast.207, bf16[4096,768]{1,0:T(8,128)(2,1)} %bitcast.6), kind=kOutput, calls=%fused_computation.176 | convolution fusion | flops 807927680 | bytes 8602112 | tf_op jit(solution)/shard_map/dot_general | solution.py:193
  294.2 1.6 pad_maximum_fusion
  296.1 31.8 %reduce-scatter.2.cloned.1.call-done = bf16[1,128,2176]{2,1,0:T(8,128)(2,1)} async-done(((bf16[4,128,2176]{2,1,0:T(8,128)(2,1)}), bf16[1,128,2176]{2,1,0:T(8,128)(2,1)}) %reduce-scatter.2.cloned.1.call-update) | async-done | bytes 557072 | tf_op jit(solution)/shard_map/reduce_scatter | solution.py:214
  329.2 1.9 fusion.29
  332.6 8.0 %collective-permute-done.8 = bf16[1,128,1024]{2,1,0:T(8,128)(2,1)S(1)} collective-permute-done((bf16[1,128,1024]{2,1,0:T(8,128)(2,1)S(1)}, bf16[1,128,1024]{2,1,0:T(8,128)(2,1)S(1)}, u32[]{:S(2)}, u32[]{:S(2)}) %collective-permute-start.8) | collective-permute-done | bytes 262176 | tf_op jit(solution)/shard_map/ppermute | solution.py:34
  341.8 11.7 %collective-permute-done.9 = bf16[2,1,128,1024]{3,2,1,0:T(8,128)(2,1)S(1)} collective-permute-done((bf16[2,1,128,1024]{3,2,1,0:T(8,128)(2,1)S(1)}, bf16[2,1,128,1024]{3,2,1,0:T(8,128)(2,1)S(1)}, u32[]{:S(2)}, u32[]{:S(2)}) %collective-permute-start.9) | collective-permute-done | bytes 524320 | tf_op jit(solution)/shard_map/ppermute | solution.py:34
  (153 shorter events, 35.7 us)
Async XLA Ops:
  11.5 12.3 %copy-start.22 = (bf16[256,64]{0,1:T(8,128)(2,1)S(1)}, bf16[256,64]{0,1:T(8,128)(2,1)}, u32[]{:S(2)}) copy-start(bf16[256,64]{0,1:T(8,128)(2,1)} %param.14) | copy-start | bytes 98308
  11.5 14.7 %copy-start.26 = (f32[3,3,256]{2,1,0:T(4,128)S(1)}, f32[3,3,256]{2,1,0:T(4,128)}, u32[]{:S(2)}) copy-start(f32[3,3,256]{2,1,0:T(4,128)} %param.11) | copy-start | bytes 27652
  11.5 186.0 %all-to-all-start = ((bf16[64,64,768]{2,1,0:T(8,128)(2,1)}), bf16[64,64,768]{2,1,0:T(8,128)(2,1)}, u32[]{:S(2)}, u32[]{:S(2)}) async-start(bf16[64,64,768]{2,1,0:T(8,128)(2,1)} %tile.9), calls=%async_computation | async-start | bytes 12582912 | tf_op jit(solution)/shard_map/all_to_all | solution.py:15
  23.9 17.4 %collective-permute-start.1 = (bf16[64,256]{1,0:T(8,128)(2,1)S(1)}, bf16[64,256]{1,0:T(8,128)(2,1)S(1)}, u32[]{:S(2)}, u32[]{:S(2)}) collective-permute-start(bf16[64,256]{1,0:T(8,128)(2,1)S(1)} %bitcast.214), channel_id=1, source_target_pairs={{0,128},{4,132},{8,136},{12,140},{16,144},{20,148},{24,152},{28,15... | collective-permute-start | bytes 98312 | tf_op jit(solution)/shard_map/ppermute | solution.py:34
  41.3 4.9 %collective-permute-start.2 = (bf16[2,64,256]{2,1,0:T(8,128)(2,1)S(1)}, bf16[2,64,256]{2,1,0:T(8,128)(2,1)S(1)}, u32[]{:S(2)}, u32[]{:S(2)}) collective-permute-start(bf16[2,64,256]{2,1,0:T(8,128)(2,1)S(1)} %maximum_select_fusion.8), channel_id=1, source_target_pairs={{0,64},{4,68},{8,72},{12,76},{16,80},{20,84},{24,88},{28,92},{32,9... | collective-permute-start | bytes 196616 | tf_op jit(solution)/shard_map/ppermute | solution.py:34
  46.2 124.2 %collective-permute-start.3 = (bf16[2,2,64,256]{3,2,0,1:T(8,128)(2,1)S(1)}, bf16[2,2,64,256]{3,2,0,1:T(8,128)(2,1)S(1)}, u32[]{:S(2)}, u32[]{:S(2)}) collective-permute-start(bf16[2,2,64,256]{3,2,0,1:T(8,128)(2,1)S(1)} %maximum_select_fusion.7), channel_id=1, source_target_pairs={{0,32},{4,36},{8,40},{12,44},{16,48},{20,52},{24,56},{28,60},{32,0... | collective-permute-start | bytes 393224 | tf_op jit(solution)/shard_map/ppermute | solution.py:34
  48.7 136.7 %copy-start.23 = (f32[128,256]{1,0:T(8,128)S(1)}, f32[128,256]{1,0:T(8,128)}, u32[]{:S(2)}) copy-start(f32[128,256]{1,0:T(8,128)} %param.12) | copy-start | bytes 393220
  170.4 12.3 %collective-permute-start.4 = (bf16[2,2,2,64,256]{4,3,0,1,2:T(8,128)(2,1)S(1)}, bf16[2,2,2,64,256]{4,3,0,1,2:T(8,128)(2,1)S(1)}, u32[]{:S(2)}, u32[]{:S(2)}) collective-permute-start(bf16[2,2,2,64,256]{4,3,0,1,2:T(8,128)(2,1)S(1)} %maximum_select_fusion.6), channel_id=1, source_target_pairs={{0,16},{4,20},{8,24},{12,28},{16,0},{20,4},{24,8},{28,12},{32,48},... | collective-permute-start | bytes 786440 | tf_op jit(solution)/shard_map/ppermute | solution.py:34
  182.8 11.6 %collective-permute-start.5 = (bf16[2,2,2,2,64,256]{5,4,0,1,2,3:T(8,128)(2,1)S(1)}, bf16[2,2,2,2,64,256]{5,4,0,1,2,3:T(8,128)(2,1)S(1)}, u32[]{:S(2)}, u32[]{:S(2)}) collective-permute-start(bf16[2,2,2,2,64,256]{5,4,0,1,2,3:T(8,128)(2,1)S(1)} %maximum_select_fusion.3), channel_id=1, source_target_pairs={{0,8},{4,12},{8,0},{12,4},{16,24},{20,28},{24,16},{28,20},{32,40},... | collective-permute-start | bytes 1572872 | tf_op jit(solution)/shard_map/ppermute | solution.py:34
  184.0 2.2 copy-start.15
  186.3 8.4 %copy-start = (bf16[128,4096]{1,0:T(8,128)(2,1)S(1)}, bf16[128,4096]{1,0:T(8,128)(2,1)}, u32[]{:S(2)}) copy-start(bf16[128,4096]{1,0:T(8,128)(2,1)} %param.8) | copy-start | bytes 3145732
  194.5 2.7 collective-permute-start.6
  195.5 12.0 %copy-start.30 = (f32[128]{0:T(128)}, f32[128]{0:T(128)S(1)}, u32[]{:S(2)}) copy-start(f32[128]{0:T(128)S(1)} %get-tuple-element.53) | copy-start | bytes 1540
  197.3 10.2 %copy-start.24 = (f32[4096]{0:T(1024)S(1)}, f32[4096]{0:T(1024)}, u32[]{:S(2)}) copy-start(f32[4096]{0:T(1024)} %param.9) | copy-start | bytes 49156
  197.5 24.4 %all-to-all-start.2 = ((f32[1,256,128]{2,0,1:T(1,128)}), f32[1,256,128]{2,0,1:T(1,128)}, u32[]{:S(2)}, u32[]{:S(2)}) async-start(f32[1,256,128]{2,0,1:T(1,128)} %bitcast.1), calls=%async_computation.2 | async-start | bytes 262144 | tf_op jit(solution)/shard_map/all_to_all | solution.py:61
  207.5 6.5 %copy-start.8 = (bf16[128,4096]{1,0:T(8,128)(2,1)S(1)}, bf16[128,4096]{1,0:T(8,128)(2,1)}, u32[]{:S(2)}) copy-start(bf16[128,4096]{1,0:T(8,128)(2,1)} %param.15) | copy-start | bytes 3145732
  212.0 7.2 %collective-permute-start = (bf16[2,3,256]{2,0,1:T(2,128)(2,1)}, bf16[2,3,256]{2,0,1:T(2,128)(2,1)S(1)}, u32[]{:S(2)}, u32[]{:S(2)}) collective-permute-start(bf16[2,3,256]{2,0,1:T(2,128)(2,1)} %bitcast.7), channel_id=1, source_target_pairs={{0,4},{4,8},{8,12},{12,16},{16,20},{20,24},{24,28},{28,32},{32,36}... | collective-permute-start | bytes 9224 | tf_op jit(solution)/shard_map/ppermute | solution.py:23
  215.5 3.9 %copy-start.9 = (f32[128,256]{1,0:T(8,128)S(1)}, f32[128,256]{1,0:T(8,128)}, u32[]{:S(2)}) copy-start(f32[128,256]{1,0:T(8,128)} %convolution_bitcast_fusion.3) | copy-start | bytes 393220
  221.9 21.1 %all-to-all-start.1 = ((f32[2,256,128]{2,0,1:T(2,128)}), f32[2,256,128]{2,0,1:T(2,128)}, u32[]{:S(2)}, u32[]{:S(2)}) async-start(f32[2,256,128]{2,0,1:T(2,128)} %copy.120), calls=%async_computation.1 | async-start | bytes 524288 | tf_op jit(solution)/shard_map/all_to_all | solution.py:61
  243.0 2.7 copy-start.10
  243.0 2.7 copy-start.11
  243.0 2.7 copy-start.12
  248.6 27.4 %copy-start.27 = (f32[256]{0:T(256)S(1)}, f32[256]{0:T(256)}, u32[]{:S(2)}) copy-start(f32[256]{0:T(256)} %param.13) | copy-start | bytes 3076
  250.2 20.7 %all-to-all-start.3 = ((f32[64,3,4,128]{3,2,1,0:T(4,128)}), f32[64,3,4,128]{3,2,1,0:T(4,128)}, u32[]{:S(2)}, u32[]{:S(2)}) async-start(f32[64,3,4,128]{3,2,1,0:T(4,128)} %copy.131), calls=%async_computation.3 | async-start | bytes 786432 | tf_op jit(solution)/shard_map/all_to_all | solution.py:69
  256.9 71.0 %reduce-scatter.2.cloned.1.call-start = ((), (), s32[]{:S(2)}) async-start(), calls=%async_computation.5 | async-start | bytes 2785280 | tf_op jit(solution)/shard_map/reduce_scatter | solution.py:214
  278.5 6.4 %collective-permute-start.7 = (f32[2,3,256]{2,0,1:T(2,128)}, f32[2,3,256]{2,0,1:T(2,128)}, u32[]{:S(2)}, u32[]{:S(2)}) collective-permute-start(f32[2,3,256]{2,0,1:T(2,128)} %slice.165), channel_id=1, source_target_pairs={{4,0},{8,4},{12,8},{16,12},{20,16},{24,20},{28,24},{32,28},{36,32}... | collective-permute-start | bytes 18440 | tf_op jit(solution)/shard_map/ppermute | solution.py:23
  291.3 2.8 copy-start.28
  295.8 33.4 %copy-start.29 = (f32[128]{0:T(128)S(1)}, f32[128]{0:T(128)}, u32[]{:S(2)}) copy-start(f32[128]{0:T(128)} %get-tuple-element.52) | copy-start | bytes 1540
  295.8 33.4 %copy-start.31 = (f32[128]{0:T(128)S(1)}, f32[128]{0:T(128)}, u32[]{:S(2)}) copy-start(f32[128]{0:T(128)} %copy-done.30) | copy-start | bytes 1540
  329.0 12.0 %copy-start.21 = (f32[1,128,64,4]{1,3,0,2:T(4,128)S(1)}, f32[1,128,64,4]{1,3,0,2:T(4,128)}, u32[]{:S(2)}) copy-start(f32[1,128,64,4]{1,3,0,2:T(4,128)} %get-tuple-element.35) | copy-start | bytes 393220
  331.1 9.5 %collective-permute-start.8 = (bf16[1,128,1024]{2,1,0:T(8,128)(2,1)S(1)}, bf16[1,128,1024]{2,1,0:T(8,128)(2,1)S(1)}, u32[]{:S(2)}, u32[]{:S(2)}) collective-permute-start(bf16[1,128,1024]{2,1,0:T(8,128)(2,1)S(1)} %bitcast.193), channel_id=1, source_target_pairs={{0,2},{1,3},{2,0},{3,1},{4,6},{5,7},{6,4},{7,5},{8,10},{9,11},{10,... | collective-permute-start | bytes 786440 | tf_op jit(solution)/shard_map/ppermute | solution.py:34
  340.7 12.8 %collective-permute-start.9 = (bf16[2,1,128,1024]{3,2,1,0:T(8,128)(2,1)S(1)}, bf16[2,1,128,1024]{3,2,1,0:T(8,128)(2,1)S(1)}, u32[]{:S(2)}, u32[]{:S(2)}) collective-permute-start(bf16[2,1,128,1024]{3,2,1,0:T(8,128)(2,1)S(1)} %maximum_select_fusion.5), channel_id=1, source_target_pairs={{0,1},{1,0},{2,3},{3,2},{4,5},{5,4},{6,7},{7,6},{8,9},{9,8},{10,11... | collective-permute-start | bytes 1572872 | tf_op jit(solution)/shard_map/ppermute | solution.py:34
  (15 other events, 17.5 us)
Sparse Core Ops, SparseCore 0:
  295.9 31.8 reduce-scatter.1
